TPU v7x, 32 devices: a whole 2x2x4 slice. The times are simulated.
32 devices in a mesh: shard: 2 (over core), tensor: 4 (over y, x), section: 4 (over z).
Axes of the slice: x: 2, y: 2, z: 4, core: 2. Of those that a mesh axis runs over, the one named last changes fastest.
Arguments:
- grad_parts: bfloat16 [2, 2304, 2304], P('shard', ('tensor', 'section')), may hold values from -1.5 to 1.5
- moment: float32 [2304, 2304], P('shard', ('tensor', 'section')), may hold values from -6 to 6
- second: float32 [2304, 2304], P('shard', ('tensor', 'section')), may hold values from 0.05 to 2
- stat_left: float32 [2304, 2304], P('shard', ('tensor', 'section')), may hold values from -0.1 to 12
- basis_left: float32 [2304, 2304], P('shard', ('tensor', 'section')), may hold values from -0.2 to 1.5
Outputs:
- update: float32 [2304, 2304], P('shard', ('tensor', 'section'))
- moment_next: float32 [2304, 2304], P('shard', ('tensor', 'section'))
- second_next: float32 [2304, 2304], P('shard', ('tensor', 'section'))
- stat_next: float32 [2304, 2304], P('shard', ('tensor', 'section'))
- basis_next: float32 [2304, 2304], P('shard', ('tensor', 'section'))
All inputs are finite; a program needn't handle non-finite values.
Results may differ from a plain program's by a relative error of at most 0.00074.
Values may be sent and summed in bfloat16 or wider, within the bound.
No kernel may reach another device: no remote copies, remote signals or barrier semaphores. Data moves between devices by JAX's collectives and lax.ppermute only.
A program may use at most 128 MiB of HBM per device.

v0:
```python
import jax
import jax.numpy as jnp
from jax import lax
from jax.sharding import PartitionSpec as P

D = 2304
NS_ITERS = 2
beta_one = 0.9
beta_two = 0.95
stat_decay = 0.95
adam_eps = 1e-08
first_fix = 1.0 - 0.9**10
second_fix = 1.0 - 0.95**10
shrink = 0.6
norm_eps = 1e-06
TS = ("tensor", "section")
PAD = 8


def exact_dot(left, right):
    return jnp.dot(left, right, precision=lax.Precision.HIGH, preferred_element_type=jnp.float32)


def contract_rows(left, right):
    return lax.dot_general(
        left,
        right,
        (((0,), (0,)), ((), ())),
        precision=lax.Precision.HIGH,
        preferred_element_type=jnp.float32,
    )


def split_bf16(x):
    top = lax.reduce_precision(x, exponent_bits=8, mantissa_bits=7)
    return (top.astype(jnp.bfloat16), (x - top).astype(jnp.bfloat16))


def bf16_dot(left, right, dims):
    return lax.dot_general(left, right, (dims, ((), ())), preferred_element_type=jnp.float32)


def split_dot(left_hi, left_lo, right, dims):
    right_hi, right_lo = split_bf16(right)
    return (
        bf16_dot(left_hi, right_hi, dims)
        + bf16_dot(left_hi, right_lo, dims)
        + bf16_dot(left_lo, right_hi, dims)
    )


def make_shards(n_shard, n_section, n_ts):
    rows = D // n_shard
    cols = D // n_ts
    assert rows % cols == 0 or cols % rows == 0
    pair = n_shard == 2

    def partner(x):
        return lax.ppermute(x, "shard", [(0, 1), (1, 0)])

    def shard_concat(x, c):
        if not pair:
            return lax.all_gather(x, "shard", axis=0, tiled=True)
        other = partner(x)
        first = jnp.where(c == 0, x, other)
        last = jnp.where(c == 0, other, x)
        return jnp.concatenate([first, last], axis=0)

    def shard_sum(x):
        if not pair:
            return lax.psum(x, "shard")
        return x + partner(x)

    def shard_sum_scatter(x, c, axis):
        if not pair:
            return lax.psum_scatter(x, "shard", scatter_dimension=axis, tiled=True)
        size = x.shape[axis] // 2
        mine = lax.dynamic_slice_in_dim(x, c * size, size, axis=axis)
        theirs = lax.dynamic_slice_in_dim(x, (1 - c) * size, size, axis=axis)
        return mine + partner(theirs)

    def block_rows(grad_rows, k, c):
        start = k * cols
        if cols <= rows:
            piece = lax.dynamic_slice_in_dim(grad_rows, start % rows, cols, axis=0)
            owner = start // rows
            if pair:
                return jnp.where(owner == c, piece, partner(piece))
            pieces = lax.all_gather(piece, "shard", axis=0, tiled=False)
            return lax.dynamic_index_in_dim(pieces, owner, axis=0, keepdims=False)
        full = lax.all_gather(grad_rows, "shard", axis=0, tiled=True)
        return lax.dynamic_slice_in_dim(full, start, cols, axis=0)

    def all_sum(value):
        x = jnp.full((PAD, 128), value, jnp.float32)
        if n_ts & n_ts - 1 == 0:
            step = 1
            while step < n_ts:
                x = x + lax.ppermute(x, TS, [(i, i ^ step) for i in range(n_ts)])
                step *= 2
        else:
            x = lax.psum(x, TS)
        return shard_sum(x)[0, 0]

    def newton_step(iterate):
        iterate_rows = lax.all_gather(iterate, TS, axis=1, tiled=True)
        z_cols = shard_sum(contract_rows(iterate_rows, iterate))
        return 1.5 * iterate - 0.5 * exact_dot(iterate_rows, z_cols)

    def shards(grad_parts, moment, second, stat_left, basis_left):
        c = lax.axis_index("shard")
        k = lax.axis_index("tensor") * n_section + lax.axis_index("section")
        part = grad_parts[0]
        if pair:
            mine = lax.dynamic_slice_in_dim(part, c * rows, rows, axis=1)
            theirs = lax.dynamic_slice_in_dim(part, (1 - c) * rows, rows, axis=1)
            grad_flip = (mine.astype(jnp.float32) + partner(theirs).astype(jnp.float32)).astype(
                jnp.bfloat16
            )
        else:
            grad_flip = lax.psum_scatter(
                part.astype(jnp.float32).astype(jnp.bfloat16),
                "shard",
                scatter_dimension=1,
                tiled=True,
            )
        grad = grad_flip.T
        grad_cols = shard_concat(grad, c)
        basis_hi, basis_lo = split_bf16(basis_left)
        stacked = lax.all_gather(jnp.stack([grad, basis_hi, basis_lo]), TS, axis=2, tiled=True)
        grad_rows, hi_rows, lo_rows = (stacked[0], stacked[1], stacked[2])
        if cols <= rows and pair:
            piece = lax.dynamic_slice(stacked, (0, k * cols % rows, 0), (1, cols, D))[0]
            grad_krows = jnp.where(k * cols // rows == c, piece, partner(piece))
        else:
            grad_krows = block_rows(grad_rows, k, c)
        gram = lax.dot_general(
            grad_rows, grad_krows, (((1,), (1,)), ((), ())), preferred_element_type=jnp.float32
        )
        stat_next = stat_decay * stat_left + (1.0 - stat_decay) / D * gram
        by_rows = ((1,), (0,))
        stat_hi, stat_lo = split_bf16(shard_concat(stat_next, c))
        quads = bf16_dot(stacked[1:], jnp.concatenate([stat_hi, stat_lo], axis=1), ((2,), (0,)))
        power = quads[0, :, :cols] + quads[0, :, cols:] + quads[1, :, :cols]
        power, stacked_later = lax.optimization_barrier((power, stacked))
        hi_later, lo_later = (stacked_later[1], stacked_later[2])
        rotated = bf16_dot(hi_later, grad_cols, by_rows) + bf16_dot(lo_later, grad_cols, by_rows)
        moment_next = beta_one * moment + (1.0 - beta_one) * rotated
        second_next = beta_two * second + (1.0 - beta_two) * rotated * rotated
        ratio = moment_next / first_fix / (jnp.sqrt(second_next / second_fix) + adam_eps)
        update = shard_sum_scatter(split_dot(hi_later, lo_later, ratio, ((0,), (0,))), c, 0)
        power_rows = lax.all_gather(power, TS, axis=1, tiled=True)
        total_sq = all_sum(jnp.sum(power * power))
        power_rows, update, total_sq = lax.optimization_barrier((power_rows, update, total_sq))
        z_cols = shard_sum(contract_rows(power_rows, power))
        scale = shrink * jnp.sqrt(D / (total_sq + norm_eps))
        iterate = 1.5 * scale * power - 0.5 * scale * scale * scale * exact_dot(power_rows, z_cols)
        for turn in range(NS_ITERS - 1):
            iterate = newton_step(iterate)
        return (update, moment_next, second_next, stat_next, iterate)

    return shards


def solution(mesh):
    n_shard = mesh.shape["shard"]
    n_section = mesh.shape["section"]
    n_ts = mesh.shape["tensor"] * n_section
    in_specs = (
        P("shard", TS, None),
        P("shard", TS),
        P("shard", TS),
        P("shard", TS),
        P("shard", TS),
    )
    out_specs = (P("shard", TS), P("shard", TS), P("shard", TS), P("shard", TS), P("shard", TS))
    return jax.shard_map(
        make_shards(n_shard, n_section, n_ts),
        mesh=mesh,
        in_specs=in_specs,
        out_specs=out_specs,
        check_vma=False,
    )
```

profile of v0, /device:TPU:0, one launch (start us, length us, event | category | flops | bytes accessed | tf_op | source)
XLA Modules:
  0.0 523.1 jit_solution(11538976663344151876)
XLA Ops:
  12.3 186.3 %all-gather.4.cloned.1.call-done = bf16[3,1152,2304]{1,2,0:T(8,128)(2,1)} async-done(((bf16[3,1152,144]{1,2,0:T(8,128)(2,1)}), bf16[3,1152,2304]{1,2,0:T(8,128)(2,1)}) %all-gather.4.cloned.1.call-update) | async-done | bytes 15925264 | tf_op jit(solution)/shard_map/all_gather | solution.py:130
  198.6 2.0 constant_dynamic-slice_fusion.1
  201.3 2.1 collective-permute-done.1
  203.4 3.6 fusion.28
  207.3 2.0 collective-permute-done.2
  209.5 6.4 %fusion = f32[2,1152,288]{1,2,0:T(8,128)S(1)} fusion(bf16[3,1152,2304]{1,2,0:T(8,128)(2,1)} %all-gather.4.cloned.1.call-done, bf16[2304,144]{0,1:T(8,128)(2,1)S(1)} %get-tuple-element.16, bf16[2304,144]{0,1:T(8,128)(2,1)S(1)} %get-tuple-element.15), kind=kOutput, calls=%fused_computation | convolution fusion | flops 3060301824 | bytes 14598144 | tf_op jit(solution)/shard_map/dot_general | solution.py:40
  217.3 1.5 collective-permute-done.3
  218.9 3.7 fusion.5
  222.6 5.0 multiply_add_fusion
  227.7 5.0 fusion.7
  232.7 2.0 fusion.18
  234.7 2.0 fusion.21
  238.5 3.6 collective-permute-done.5
  244.2 3.2 collective-permute-done.6
  249.5 2.3 collective-permute-done.7
  253.2 2.2 collective-permute-done.8
  258.1 90.8 %all-gather.6.cloned.1.call-done = f32[1152,2304]{0,1:T(8,128)} async-done(((f32[1152,144]{0,1:T(8,128)}), f32[1152,2304]{0,1:T(8,128)}) %all-gather.6.cloned.1.call-update) | async-done | bytes 10616848 | tf_op jit(solution)/shard_map/all_gather | solution.py:152
  348.8 8.4 %fusion.53 = f32[2304,144]{0,1:T(8,128)S(1)} fusion(f32[1152,2304]{0,1:T(8,128)} %all-gather.6.cloned.1.call-done, f32[1152,144]{0,1:T(8,128)S(1)} %copy-done.1), kind=kOutput, calls=%fused_computation.74 | convolution fusion | flops 2293235712 | bytes 12607488 | tf_op jit(solution)/shard_map/dot_general | solution.py:25
  358.0 2.3 collective-permute-done.10
  360.4 8.3 %fusion.29 = f32[1152,144]{0,1:T(8,128)} fusion(f32[1152,2304]{0,1:T(8,128)} %all-gather.6.cloned.1.call-done, f32[2304,144]{0,1:T(8,128)S(1)} %fusion.53, f32[2304,144]{0,1:T(8,128)S(1)} %collective-permute-done.10, f32[1152,144]{0,1:T(8,128)S(1)} %copy-done.1, f32[]{:T(128)S(6)} %mul.108, f32[]{:T(128)S(6)} %mul.103), kind=kOutput, calls=%fused_computation.26 | convolution fusion | flops 2294065152 | bytes 14598152 | tf_op jit(solution)/shard_map/dot_general | solution.py:21
  368.6 131.8 %all-gather.8.cloned.1.call-done = f32[1152,2304]{0,1:T(8,128)} async-done(((f32[1152,144]{0,1:T(8,128)}), f32[1152,2304]{0,1:T(8,128)}) %all-gather.8.cloned.1.call-update) | async-done | bytes 10616848 | tf_op jit(solution)/shard_map/all_gather | solution.py:106
  500.4 8.6 %fusion.54 = f32[2304,144]{0,1:T(8,128)S(1)} fusion(f32[1152,2304]{0,1:T(8,128)} %all-gather.8.cloned.1.call-done, f32[1152,144]{0,1:T(8,128)} %fusion.29), kind=kOutput, calls=%fused_computation.75 | convolution fusion | flops 2293235712 | bytes 12607488 | tf_op jit(solution)/shard_map/dot_general | solution.py:25
  509.2 3.0 collective-permute-done.11
  512.2 4.3 multiply_subtract_fusion
  (67 shorter events, 17.8 us)
Async XLA Ops:
  7.2 191.5 %all-gather.4.cloned.1.call-start = ((), (), s32[]{:S(2)}) async-start(), calls=%async_computation | async-start | bytes 16920576 | tf_op jit(solution)/shard_map/all_gather | solution.py:130
  8.2 1.8 collective-permute-start
  12.2 191.2 %copy-start.4 = (f32[1152,144]{0,1:T(8,128)S(1)}, f32[1152,144]{0,1:T(8,128)}, u32[]{:S(2)}) copy-start(f32[1152,144]{0,1:T(8,128)} %param.8) | copy-start | bytes 1990660
  12.2 336.6 %all-gather.6.cloned.1.call-start = ((), (), s32[]{:S(2)}) async-start(), calls=%async_computation.1 | async-start | bytes 11280384 | tf_op jit(solution)/shard_map/all_gather | solution.py:152
  201.2 2.2 collective-permute-start.1
  207.1 2.2 collective-permute-start.2
  216.8 283.6 %all-gather.8.cloned.1.call-start = ((), (), s32[]{:S(2)}) async-start(), calls=%async_computation.2 | async-start | bytes 11280384 | tf_op jit(solution)/shard_map/all_gather | solution.py:106
  217.1 1.7 collective-permute-start.3
  218.8 13.8 %slice-start = ((s8[15925248]{0:T(1024)(128)(4,1)}), s8[4194304]{0:T(1024)(128)(4,1)S(1)}, s32[]{:S(2)}) async-start(s8[15925248]{0:T(1024)(128)(4,1)} %bitcast.63), calls=%async_computation.3 | async-start | bytes 8388608
  218.9 13.8 %slice-start.1 = ((s8[15925248]{0:T(1024)(128)(4,1)}), s8[4194304]{0:T(1024)(128)(4,1)S(1)}, s32[]{:S(2)}) async-start(s8[15925248]{0:T(1024)(128)(4,1)} %bitcast.63), calls=%async_computation.4 | async-start | bytes 8388608
  222.6 10.1 %slice-start.2 = ((s8[15925248]{0:T(1024)(128)(4,1)}), s8[4194304]{0:T(1024)(128)(4,1)S(1)}, s32[]{:S(2)}) async-start(s8[15925248]{0:T(1024)(128)(4,1)} %bitcast.63), calls=%async_computation.5 | async-start | bytes 8388608
  227.6 7.1 %copy-start.7 = (f32[1152,144]{0,1:T(8,128)}, f32[1152,144]{0,1:T(8,128)S(1)}, u32[]{:S(2)}) copy-start(f32[1152,144]{0,1:T(8,128)S(1)} %get-tuple-element.21) | copy-start | bytes 1990660
  227.6 7.1 %copy-start.8 = (f32[1152,144]{0,1:T(8,128)}, f32[1152,144]{0,1:T(8,128)S(1)}, u32[]{:S(2)}) copy-start(f32[1152,144]{0,1:T(8,128)S(1)} %get-tuple-element.22) | copy-start | bytes 1990660
  227.6 5.1 slice-start.3
  236.8 20.3 %collective-permute-start.4 = (f32[1152,144]{0,1:T(8,128)S(1)}, f32[1152,144]{0,1:T(8,128)S(1)}, u32[]{:S(2)}, u32[]{:S(2)}) collective-permute-start(f32[1152,144]{0,1:T(8,128)S(1)} %constant_dynamic-slice_fusion), channel_id=1, source_target_pairs={{0,16},{16,0},{1,17},{17,1},{2,18},{18,2},{3,19},{19,3},{4,20},{20... | collective-permute-start | bytes 1990664 | tf_op jit(solution)/shard_map/ppermute | solution.py:59
  238.4 3.7 collective-permute-start.5
  242.8 4.6 collective-permute-start.6
  248.0 3.7 collective-permute-start.7
  251.7 3.7 collective-permute-start.8
  255.4 1.2 collective-permute-start.9
  357.2 3.1 collective-permute-start.10
  368.6 143.6 %copy-start.2 = (f32[1152,144]{0,1:T(8,128)S(1)}, f32[1152,144]{0,1:T(8,128)}, u32[]{:S(2)}) copy-start(f32[1152,144]{0,1:T(8,128)} %fusion.29) | copy-start | bytes 1990660
  500.4 11.8 %copy-start = (f32[1152,2304]{0,1:T(8,128)S(1)}, f32[1152,2304]{0,1:T(8,128)}, u32[]{:S(2)}) copy-start(f32[1152,2304]{0,1:T(8,128)} %all-gather.8.cloned.1.call-done) | copy-start | bytes 31850500
  509.1 3.1 collective-permute-start.11
  (4 other events, 12.3 us)
Sparse Core Ops, SparseCore 0:
  12.3 186.2 all-gather.3
  217.0 131.8 all-gather.5
  368.8 131.6 all-gather.7
where the time goes:
time: 524 us; the launch traced here: 523 us
  waiting for transfers between devices  432 us (82%)
  matrix products  57.4 us (11%)
  between operations  14.8 us (3%)
  other arithmetic  7.58 us (1%)
  starting transfers between devices  6.04 us (1%)
    all_gather x1, waiting for transfers between devices, shards(): lax.all_gather(jnp.stack([grad, basis_hi, basis_lo]), TS, axis=2, tiled=T...  186 us
    all_gather x1, waiting for transfers between devices, newton_step(): iterate_rows = lax.all_gather(iterate, TS, axis=1, tiled=True)  132 us
    all_gather x1, waiting for transfers between devices, shards(): power_rows = lax.all_gather(power, TS, axis=1, tiled=True)  90.8 us
    dot_general x6, matrix products, bf16_dot(): lax.dot_general(left, right, (dims, ((), ())), preferred_element_type=jnp...  24.1 us
    dot_general x2, matrix products, contract_rows(): lax.dot_general(left, right, (((0,), (0,)), ((), ())), precision=lax.Prec...  17.1 us
    dot_general x2, matrix products, exact_dot(): jnp.dot(left, right, precision=lax.Precision.HIGH, preferred_element_type...  12.6 us
    ppermute x8, waiting for transfers between devices, partner(): return lax.ppermute(x, 'shard', [(0, 1), (1, 0)])  12.2 us
    ppermute x4, waiting for transfers between devices, all_sum(): x = x + lax.ppermute(x, TS, [(i, i ^ step) for i in range(n_ts)])  11.2 us
  transfers between devices with their start and end apart: 15, of which 14 were waited for; matrix products, arithmetic and copies ran while one was open for 4% of the time, Pallas kernels for 0%

commit v1 on v0

--- a/solution.py
+++ b/solution.py
@@ -103,7 +103,14 @@
         return shard_sum(x)[0, 0]
 
     def newton_step(iterate):
-        iterate_rows = lax.all_gather(iterate, TS, axis=1, tiled=True)
+        ways, here = (lax.axis_size(TS), lax.axis_index(TS))
+        iterate_rows, reach = (iterate, 1)
+        while reach < ways:
+            received = lax.ppermute(iterate_rows, TS, [(d, d ^ reach) for d in range(ways)])
+            mine_first = jnp.concatenate([iterate_rows, received], axis=1)
+            theirs_first = jnp.concatenate([received, iterate_rows], axis=1)
+            iterate_rows = jnp.where(here & reach == 0, mine_first, theirs_first)
+            reach = 2 * reach
         z_cols = shard_sum(contract_rows(iterate_rows, iterate))
         return 1.5 * iterate - 0.5 * exact_dot(iterate_rows, z_cols)
 

time: 524 us -> 661 us (1.26)
  waiting for transfers between devices: 432 us -> 549 us
  other arithmetic: 7.58 us -> 16 us
  matrix products: 57.4 us -> 65.6 us
    ppermute x0 -> x4, waiting for transfers between devices: none -> 248 us  [newton_step(): lax.ppermute(iterate_rows, TS, [(d, d ^ reach) for d in range(ways)])]
    all_gather x1 -> x0, waiting for transfers between devices: 132 us -> none  [newton_step(): iterate_rows = lax.all_gather(iterate, TS, axis=1, tiled=True)]
    select_n x0 -> x3, other arithmetic: none -> 8.3 us  [newton_step(): iterate_rows = jnp.where(here & reach == 0, mine_first, theirs_first)]
    dot_general x2, matrix products: 12.6 us -> 19.3 us  [exact_dot(): jnp.dot(left, right, precision=lax.Precision.HIGH, preferred_element_type...]
  transfers between devices with their start and end apart: 15 -> 18, of which waited for: 14 -> 17; matrix products, arithmetic and copies ran while one was open for 4% -> 4% of each run, Pallas kernels for 0% -> 0%
where the time goes in v1:
time: 661 us
  waiting for transfers between devices  549 us (83%)
  matrix products  65.6 us (10%)
  other arithmetic  16 us (2%)
  between operations  15.2 us (2%)
  starting transfers between devices  10.3 us (2%)
    ppermute x4, waiting for transfers between devices, newton_step(): lax.ppermute(iterate_rows, TS, [(d, d ^ reach) for d in range(ways)])  248 us
    all_gather x1, waiting for transfers between devices, shards(): lax.all_gather(jnp.stack([grad, basis_hi, basis_lo]), TS, axis=2, tiled=T...  186 us
    all_gather x1, waiting for transfers between devices, shards(): power_rows = lax.all_gather(power, TS, axis=1, tiled=True)  90.9 us
    dot_general x6, matrix products, bf16_dot(): lax.dot_general(left, right, (dims, ((), ())), preferred_element_type=jnp...  24.2 us
    dot_general x2, matrix products, exact_dot(): jnp.dot(left, right, precision=lax.Precision.HIGH, preferred_element_type...  19.3 us
    dot_general x2, matrix products, contract_rows(): lax.dot_general(left, right, (((0,), (0,)), ((), ())), precision=lax.Prec...  18.4 us
  transfers between devices with their start and end apart: 18, of which 17 were waited for; matrix products, arithmetic and copies ran while one was open for 4% of the time, Pallas kernels for 0%

profile of v1, /device:TPU:0, one launch (start us, length us, event | category | flops | bytes accessed | tf_op | source)
XLA Modules:
  0.0 660.6 jit_solution(4364683551532801337)
XLA Ops:
  12.3 186.3 %all-gather.3.cloned.1.call-done = bf16[3,1152,2304]{1,2,0:T(8,128)(2,1)} async-done(((bf16[3,1152,144]{1,2,0:T(8,128)(2,1)}), bf16[3,1152,2304]{1,2,0:T(8,128)(2,1)}) %all-gather.3.cloned.1.call-update) | async-done | bytes 15925264 | tf_op jit(solution)/shard_map/all_gather | solution.py:137
  201.3 2.1 collective-permute-done.1
  203.4 3.6 fusion.32
  209.6 6.6 fusion
  218.9 3.7 fusion.7
  222.6 5.0 multiply_add_fusion
  227.7 5.0 fusion.9
  238.5 3.6 collective-permute-done.5
  244.1 3.2 collective-permute-done.6
  249.4 2.3 collective-permute-done.7
  253.1 2.3 collective-permute-done.8
  258.1 90.9 %all-gather.5.cloned.1.call-done = f32[1152,2304]{0,1:T(8,128)} async-done(((f32[1152,144]{0,1:T(8,128)}), f32[1152,2304]{0,1:T(8,128)}) %all-gather.5.cloned.1.call-update) | async-done | bytes 10616848 | tf_op jit(solution)/shard_map/all_gather | solution.py:159
  349.0 8.4 %fusion.60 = f32[2304,144]{0,1:T(8,128)S(1)} fusion(f32[1152,2304]{0,1:T(8,128)} %all-gather.5.cloned.1.call-done, f32[1152,144]{0,1:T(8,128)S(1)} %copy-done), kind=kOutput, calls=%fused_computation.84 | convolution fusion | flops 2293235712 | bytes 12607488 | tf_op jit(solution)/shard_map/dot_general | solution.py:25
  358.2 2.5 collective-permute-done.10
  360.7 7.7 %fusion.34 = f32[1152,144]{0,1:T(8,128)S(1)} fusion(f32[1152,2304]{0,1:T(8,128)} %all-gather.5.cloned.1.call-done, f32[2304,144]{0,1:T(8,128)S(1)} %fusion.60, f32[2304,144]{0,1:T(8,128)} %collective-permute-done.10, f32[1152,144]{0,1:T(8,128)S(1)} %copy-done, f32[]{:T(128)S(6)} %mul.109, f32[]{:T(128)S(6)} %mul.104), kind=kOutput, calls=%fused_computation.33 | convolution fusion | flops 2294065152 | bytes 14598152 | tf_op jit(solution)/shard_map/dot_general | solution.py:21
  368.5 16.9 %collective-permute-done.11 = f32[1152,144]{0,1:T(8,128)S(1)} collective-permute-done((f32[1152,144]{0,1:T(8,128)S(1)}, f32[1152,144]{0,1:T(8,128)S(1)}, u32[]{:S(2)}, u32[]{:S(2)}) %collective-permute-start.11) | collective-permute-done | bytes 663584 | tf_op jit(solution)/shard_map/ppermute | solution.py:109
  387.1 58.3 %collective-permute-done.12 = f32[1152,288]{0,1:T(8,128)} collective-permute-done((f32[1152,288]{0,1:T(8,128)S(1)}, f32[1152,288]{0,1:T(8,128)}, u32[]{:S(2)}, u32[]{:S(2)}) %collective-permute-start.12) | collective-permute-done | bytes 1327136 | tf_op jit(solution)/shard_map/ppermute | solution.py:109
  445.4 2.8 maximum_select_fusion.4
  449.7 58.1 %collective-permute-done.13 = f32[1152,576]{0,1:T(8,128)} collective-permute-done((f32[1152,576]{0,1:T(8,128)S(1)}, f32[1152,576]{0,1:T(8,128)}, u32[]{:S(2)}, u32[]{:S(2)}) %collective-permute-start.13) | collective-permute-done | bytes 2654240 | tf_op jit(solution)/shard_map/ppermute | solution.py:109
  507.8 5.4 maximum_select_fusion.3
  514.7 114.3 %collective-permute-done.14 = f32[1152,1152]{0,1:T(8,128)} collective-permute-done((f32[1152,1152]{0,1:T(8,128)}, f32[1152,1152]{0,1:T(8,128)}, u32[]{:S(2)}, u32[]{:S(2)}) %collective-permute-start.14) | collective-permute-done | bytes 5308448 | tf_op jit(solution)/shard_map/ppermute | solution.py:109
  629.0 10.0 %fusion.3 = f32[2304,144]{0,1:T(8,128)S(1)} fusion(f32[1152,144]{0,1:T(8,128)S(1)} %fusion.34, f32[1152,1152]{0,1:T(8,128)} %collective-permute-done.14, f32[1152,1152]{0,1:T(8,128)} %maximum_select_fusion.3, pred[]{:T(512)S(6)} %eq.25), kind=kOutput, calls=%fused_computation.4 | convolution fusion | flops 2301198336 | bytes 12607489 | tf_op jit(solution)/shard_map/dot_general | solution.py:25
  639.1 3.0 collective-permute-done.15
  642.1 11.6 %multiply_subtract_fusion = f32[1152,144]{0,1:T(8,128)} fusion(f32[1152,144]{0,1:T(8,128)S(1)} %fusion.34, f32[2304,144]{0,1:T(8,128)S(1)} %fusion.3, f32[2304,144]{0,1:T(8,128)S(1)} %collective-permute-done.15, f32[1152,1152]{0,1:T(8,128)} %collective-permute-done.14, f32[1152,1152]{0,1:T(8,128)} %maximum_select_fusion.3, pred[]{:T(512)S(6)} %eq.25), kind=kOutput, calls=%fused_computation.59 | convolution fusion | flops 2302027776 | bytes 14598145 | tf_op jit(solution)/shard_map/dot_general | solution.py:21
  (73 shorter events, 31.7 us)
Async XLA Ops:
  7.2 191.5 %all-gather.3.cloned.1.call-start = ((), (), s32[]{:S(2)}) async-start(), calls=%async_computation | async-start | bytes 16920576 | tf_op jit(solution)/shard_map/all_gather | solution.py:137
  8.2 1.8 collective-permute-start
  12.2 191.2 %copy-start.3 = (f32[1152,144]{0,1:T(8,128)S(1)}, f32[1152,144]{0,1:T(8,128)}, u32[]{:S(2)}) copy-start(f32[1152,144]{0,1:T(8,128)} %param.8) | copy-start | bytes 1990660
  12.2 336.8 %all-gather.5.cloned.1.call-start = ((), (), s32[]{:S(2)}) async-start(), calls=%async_computation.1 | async-start | bytes 11280384 | tf_op jit(solution)/shard_map/all_gather | solution.py:159
  201.2 2.2 collective-permute-start.1
  207.1 2.2 collective-permute-start.2
  217.1 1.7 collective-permute-start.3
  218.9 13.8 %slice-start = ((s8[15925248]{0:T(1024)(128)(4,1)}), s8[4194304]{0:T(1024)(128)(4,1)S(1)}, s32[]{:S(2)}) async-start(s8[15925248]{0:T(1024)(128)(4,1)} %bitcast.61), calls=%async_computation.2 | async-start | bytes 8388608
  218.9 13.8 %slice-start.1 = ((s8[15925248]{0:T(1024)(128)(4,1)}), s8[4194304]{0:T(1024)(128)(4,1)S(1)}, s32[]{:S(2)}) async-start(s8[15925248]{0:T(1024)(128)(4,1)} %bitcast.61), calls=%async_computation.3 | async-start | bytes 8388608
  222.6 10.1 %slice-start.2 = ((s8[15925248]{0:T(1024)(128)(4,1)}), s8[4194304]{0:T(1024)(128)(4,1)S(1)}, s32[]{:S(2)}) async-start(s8[15925248]{0:T(1024)(128)(4,1)} %bitcast.61), calls=%async_computation.4 | async-start | bytes 8388608
  227.6 7.1 %copy-start.6 = (f32[1152,144]{0,1:T(8,128)}, f32[1152,144]{0,1:T(8,128)S(1)}, u32[]{:S(2)}) copy-start(f32[1152,144]{0,1:T(8,128)S(1)} %get-tuple-element.21) | copy-start | bytes 1990660
  227.6 7.1 %copy-start.7 = (f32[1152,144]{0,1:T(8,128)}, f32[1152,144]{0,1:T(8,128)S(1)}, u32[]{:S(2)}) copy-start(f32[1152,144]{0,1:T(8,128)S(1)} %get-tuple-element.22) | copy-start | bytes 1990660
  236.8 20.4 %collective-permute-start.4 = (f32[1152,144]{0,1:T(8,128)S(1)}, f32[1152,144]{0,1:T(8,128)S(1)}, u32[]{:S(2)}, u32[]{:S(2)}) collective-permute-start(f32[1152,144]{0,1:T(8,128)S(1)} %constant_dynamic-slice_fusion), channel_id=1, source_target_pairs={{0,16},{16,0},{1,17},{17,1},{2,18},{18,2},{3,19},{19,3},{4,20},{20... | collective-permute-start | bytes 1990664 | tf_op jit(solution)/shard_map/ppermute | solution.py:59
  238.4 3.7 collective-permute-start.5
  242.8 4.6 collective-permute-start.6
  248.0 3.7 collective-permute-start.7
  251.7 3.7 collective-permute-start.8
  255.4 1.2 collective-permute-start.9
  357.4 3.3 collective-permute-start.10
  368.4 17.0 %collective-permute-start.11 = (f32[1152,144]{0,1:T(8,128)S(1)}, f32[1152,144]{0,1:T(8,128)S(1)}, u32[]{:S(2)}, u32[]{:S(2)}) collective-permute-start(f32[1152,144]{0,1:T(8,128)S(1)} %fusion.34), channel_id=1, source_target_pairs={{0,1},{1,0},{2,3},{3,2},{4,5},{5,4},{6,7},{7,6},{8,9},{9,8},{10,11... | collective-permute-start | bytes 1990664 | tf_op jit(solution)/shard_map/ppermute | solution.py:109
  385.5 59.9 %collective-permute-start.12 = (f32[1152,288]{0,1:T(8,128)S(1)}, f32[1152,288]{0,1:T(8,128)}, u32[]{:S(2)}, u32[]{:S(2)}) collective-permute-start(f32[1152,288]{0,1:T(8,128)S(1)} %maximum_select_fusion.7), channel_id=1, source_target_pairs={{0,2},{1,3},{2,0},{3,1},{4,6},{5,7},{6,4},{7,5},{8,10},{9,11},{10,... | collective-permute-start | bytes 3981320 | tf_op jit(solution)/shard_map/ppermute | solution.py:109
  448.2 59.6 %collective-permute-start.13 = (f32[1152,576]{0,1:T(8,128)S(1)}, f32[1152,576]{0,1:T(8,128)}, u32[]{:S(2)}, u32[]{:S(2)}) collective-permute-start(f32[1152,576]{0,1:T(8,128)S(1)} %maximum_select_fusion.4), channel_id=1, source_target_pairs={{0,4},{1,5},{2,6},{3,7},{4,0},{5,1},{6,2},{7,3},{8,12},{9,13},{10,... | collective-permute-start | bytes 7962632 | tf_op jit(solution)/shard_map/ppermute | solution.py:109
  513.2 115.8 %collective-permute-start.14 = (f32[1152,1152]{0,1:T(8,128)}, f32[1152,1152]{0,1:T(8,128)}, u32[]{:S(2)}, u32[]{:S(2)}) collective-permute-start(f32[1152,1152]{0,1:T(8,128)} %maximum_select_fusion.3), channel_id=1, source_target_pairs={{0,8},{1,9},{2,10},{3,11},{4,12},{5,13},{6,14},{7,15},{8,0},{9,1},... | collective-permute-start | bytes 15925256 | tf_op jit(solution)/shard_map/ppermute | solution.py:109
  639.0 3.1 collective-permute-start.15
  (6 other events, 19.1 us)
Sparse Core Ops, SparseCore 0:
  12.3 186.2 all-gather.2
  217.2 131.7 all-gather.4
